TPU v7x, 512 devices: a whole 4x8x8 slice. The times are simulated.
512 devices in a mesh: dp: 8 (over y_lo, core), gx: 64 (over y_hi, z, x).
Axes of the slice: x: 4, y: 8 (y_hi: 2, y_lo: 4; y = y_hi * 4 + y_lo), z: 8, core: 2. Of those that a mesh axis runs over, the one named last changes fastest.
Arguments:
- features: bfloat16 [8, 16, 128, 8, 256], P('dp', None, 'gx'), may hold values from -6 to 6
- offsets: int32 [8, 3], P('dp'), may hold values from 0 to 255, as said below
- flip_bits: int32 [8, 3], P('dp'), may hold values from 0 to 1
- weight: bfloat16 [27, 16, 16], replicated, may hold values from -0.3125 to 0.3125
- conv_bias: float32 [16], replicated, may hold values from -3 to 3
- cotangent: bfloat16 [8, 16, 128, 8, 256], P('dp', None, 'gx'), may hold values from -6 to 6
Outputs:
- hidden: bfloat16 [8, 16, 128, 8, 256], P('dp', None, 'gx')
- grad_input: bfloat16 [8, 16, 128, 8, 256], P('dp', None, 'gx')
- grad_weight: float32 [27, 16, 16], replicated
- grad_bias: float32 [16], replicated
Inputs may be any that keep to these rules, and one draw needn't show every extreme that they name: `offsets`: column 0 lies in 0 to 127, column 1 in 0 to 7, column 2 in 0 to 255.
All inputs are finite; a program needn't handle non-finite values.
Results may differ from a plain program's by a relative error of at most 0.0075.
Values may be sent and summed in bfloat16 or wider, within the bound.
No kernel may reach another device: no remote copies, remote signals or barrier semaphores. Data moves between devices by JAX's collectives and lax.ppermute only.
A program may use at most 64 MiB of HBM per device.

v0:
```python
import math
import jax
import jax.numpy as jnp
from jax import lax
from jax.sharding import PartitionSpec as P

tap_offsets = [
    (shift_x, shift_y, shift_z)
    for shift_x in range(3)
    for shift_y in range(3)
    for shift_z in range(3)
]


def partner_2(block, axis, bit):
    count = lax.axis_size(axis)
    route = []
    for low in range(count):
        high = low | 1 << bit
        if high != low and high < count:
            route += [(low, high), (high, low)]
    return lax.ppermute(block, axis, route)


def shifted(value, axis, steps):
    count = lax.axis_size(axis)
    pairs = [(source, (source + steps) % count) for source in range(count)]
    return lax.ppermute(value, axis, pairs)


def padded_2(shard, sides, width):
    for axis, dim in sides:
        peers, length = (lax.axis_size(axis), shard.shape[dim])
        up = [(i, (i + 1) % peers) for i in range(peers)]
        down = [(j, i) for i, j in up]
        last = lax.slice_in_dim(shard, length - width, length, axis=dim)
        leading = lax.slice_in_dim(shard, 0, width, axis=dim)
        before = lax.ppermute(last, axis, up)
        after = lax.ppermute(leading, axis, down)
        shard = jnp.concatenate([before, shard, after], axis=dim)
    return shard


def permute_axis(volume, offset, mirror_bit, length, dim_index):
    position = jnp.arange(length, dtype=jnp.int32)
    source = jnp.where(mirror_bit == 1, length - 1 - position, position)
    source = jnp.mod(source - offset, length)
    return jnp.take(volume, source, axis=dim_index)


def augment_local(volume, offset, mirror_bits):
    volume = permute_axis(volume, offset[1], mirror_bits[1], volume.shape[2], 2)
    return permute_axis(volume, offset[2], mirror_bits[2], volume.shape[3], 3)


def gelu_parts(pre_act):
    normal_cdf = 0.5 * (1.0 + lax.erf(pre_act * 0.7071067811865476))
    density = jnp.exp(-0.5 * pre_act * pre_act) * 0.3989422804014327
    return (pre_act * normal_cdf, normal_cdf + pre_act * density)


def cut_planes(stacked, begin_at, length):

    def single(volume, first):
        return lax.dynamic_slice_in_dim(volume, first, length, 1)

    return jax.vmap(single)(stacked, begin_at)


def on_device(features, offsets, flip_bits, weight, conv_bias, cotangent):
    planes = features.shape[2]
    devices_x = lax.axis_size("gx")
    levels = devices_x.bit_length() - 1
    length_x = planes * devices_x
    local = jax.vmap(augment_local)(features, offsets, flip_bits)
    mirror_x = (flip_bits[:, 0] == 1)[:, None, None, None, None]
    mirrored = jnp.where(mirror_x, jnp.flip(local, 2), local)
    for bit_level in range(levels):
        partner = partner_2(mirrored, "gx", bit_level)
        mirrored = jnp.where(mirror_x, partner, mirrored)
    effective = jnp.where(flip_bits[:, 0] == 1, jnp.mod(-offsets[:, 0], length_x), offsets[:, 0])
    coarse_steps = effective // planes
    remain = effective % planes
    coarse = mirrored
    for bit_level in range(levels):
        arrived = shifted(coarse, "gx", 2**bit_level)
        taken = (coarse_steps // 2**bit_level % 2 == 1)[:, None, None, None, None]
        coarse = jnp.where(taken, arrived, coarse)
    previous = shifted(coarse, "gx", 1)
    joined = jnp.concatenate([previous, coarse], axis=2)
    augmented = cut_planes(joined, planes - remain, planes)
    padded = padded_2(augmented, (("gx", 2),), 1)
    total = jnp.zeros(features.shape, jnp.float32) + conv_bias[None, :, None, None, None]
    for tap_index, (shift_x, shift_y, shift_z) in enumerate(tap_offsets):
        window = jnp.roll(
            padded[:, :, shift_x : shift_x + planes], (1 - shift_y, 1 - shift_z), axis=(3, 4)
        )
        total = total + jnp.einsum(
            "oi,bixyz->boxyz", weight[tap_index], window, preferred_element_type=jnp.float32
        )
    hidden, slope = gelu_parts(total)
    grad_pre = (cotangent.astype(jnp.float32) * slope).astype(jnp.bfloat16)
    grad_pad = padded_2(grad_pre, (("gx", 2),), 1)
    grad_in = jnp.zeros(features.shape, jnp.float32)
    grad_list = []
    for tap_index, (shift_x, shift_y, shift_z) in enumerate(tap_offsets):
        window = jnp.roll(
            padded[:, :, shift_x : shift_x + planes], (1 - shift_y, 1 - shift_z), axis=(3, 4)
        )
        grad_list.append(
            jnp.einsum("boxyz,bixyz->oi", grad_pre, window, preferred_element_type=jnp.float32)
        )
        moved_grad = jnp.roll(
            grad_pad[:, :, 2 - shift_x : 2 - shift_x + planes],
            (shift_y - 1, shift_z - 1),
            axis=(3, 4),
        )
        grad_in = grad_in + jnp.einsum(
            "oi,boxyz->bixyz", weight[tap_index], moved_grad, preferred_element_type=jnp.float32
        )
    grad_b = jnp.sum(grad_pre.astype(jnp.float32), axis=(0, 2, 3, 4))
    summed_w, summed_b = lax.psum((jnp.stack(grad_list), grad_b), ("dp", "gx"))
    cell_count = (
        features.shape[0] * lax.axis_size("dp") * length_x * features.shape[3] * features.shape[4]
    )
    grad_scale = 1.0 / math.sqrt(cell_count)
    return (
        hidden.astype(jnp.bfloat16),
        grad_in.astype(jnp.bfloat16),
        summed_w * grad_scale,
        summed_b * grad_scale,
    )


def solution(mesh):
    in_specs = (
        P("dp", None, "gx", None, None),
        P("dp", None),
        P("dp", None),
        P(),
        P(),
        P("dp", None, "gx", None, None),
    )
    out_specs = (P("dp", None, "gx", None, None), P("dp", None, "gx", None, None), P(), P())
    return jax.shard_map(
        on_device, mesh=mesh, in_specs=in_specs, out_specs=out_specs, check_vma=False
    )
```

profile of v0, /device:TPU:1, one launch (start us, length us, event | category | flops | bytes accessed | tf_op | source)
XLA Modules:
  0.0 339.2 jit_solution(17937598453677583954)
XLA Ops:
  0.6 1.4 fusion.388
  2.1 1.4 fusion.389
  4.1 0.7 compare_and_fusion.1
  4.7 0.7 compare_select_fusion
  6.0 0.6 compare_select_fusion.4
  6.7 0.6 compare_and_fusion
  8.0 0.9 gather_fusion
  9.1 0.6 copy.69
  9.6 0.9 gather_fusion.1
  10.6 0.8 copy.70
  11.5 3.9 %collective-permute-start = (bf16[1,16,2,8,256]{4,1,3,2,0:T(8,128)(2,1)S(1)}, bf16[1,16,2,8,256]{4,1,3,2,0:T(8,128)(2,1)S(1)}, u32[]{:S(2)}, u32[]{:S(2)}) collective-permute-start(bf16[1,16,2,8,256]{4,1,3,2,0:T(8,128)(2,1)S(1)} %reverse_select_fusion), channel_id=1, source_target_pairs={{0,1},{1,0},{2,3},{3,2},{4,5},{5,4},{6,7},{7,6},{8,9},{9,8},{10,11... | collective-permute-start | bytes 393224 | tf_op jit(solution)/shard_map/ppermute | solution.py:22
  15.4 2.3 collective-permute-done
  17.8 5.4 %collective-permute-start.1 = (bf16[1,16,2,8,256]{4,1,3,2,0:T(8,128)(2,1)S(1)}, bf16[1,16,2,8,256]{4,1,3,2,0:T(8,128)(2,1)S(1)}, u32[]{:S(2)}, u32[]{:S(2)}) collective-permute-start(bf16[1,16,2,8,256]{4,1,3,2,0:T(8,128)(2,1)S(1)} %broadcast_select_fusion.5), channel_id=1, source_target_pairs={{0,2},{2,0},{1,3},{3,1},{4,6},{6,4},{5,7},{7,5},{8,10},{10,8},{9,1... | collective-permute-start | bytes 393224 | tf_op jit(solution)/shard_map/ppermute | solution.py:22
  23.3 2.3 collective-permute-done.1
  25.6 4.2 %collective-permute-start.2 = (bf16[1,16,2,8,256]{4,1,3,2,0:T(8,128)(2,1)S(1)}, bf16[1,16,2,8,256]{4,1,3,2,0:T(8,128)(2,1)S(1)}, u32[]{:S(2)}, u32[]{:S(2)}) collective-permute-start(bf16[1,16,2,8,256]{4,1,3,2,0:T(8,128)(2,1)S(1)} %broadcast_select_fusion.4), channel_id=1, source_target_pairs={{0,4},{4,0},{1,5},{5,1},{2,6},{6,2},{3,7},{7,3},{8,12},{12,8},{9,1... | collective-permute-start | bytes 393224 | tf_op jit(solution)/shard_map/ppermute | solution.py:22
  29.9 2.6 collective-permute-done.2
  32.5 5.5 %collective-permute-start.3 = (bf16[1,16,2,8,256]{4,1,3,2,0:T(8,128)(2,1)S(1)}, bf16[1,16,2,8,256]{4,1,3,2,0:T(8,128)(2,1)S(1)}, u32[]{:S(2)}, u32[]{:S(2)}) collective-permute-start(bf16[1,16,2,8,256]{4,1,3,2,0:T(8,128)(2,1)S(1)} %broadcast_select_fusion.3), channel_id=1, source_target_pairs={{0,8},{8,0},{1,9},{9,1},{2,10},{10,2},{3,11},{11,3},{4,12},{12,4},... | collective-permute-start | bytes 393224 | tf_op jit(solution)/shard_map/ppermute | solution.py:22
  38.0 3.8 %collective-permute-done.3 = bf16[1,16,2,8,256]{4,1,3,2,0:T(8,128)(2,1)S(1)} collective-permute-done((bf16[1,16,2,8,256]{4,1,3,2,0:T(8,128)(2,1)S(1)}, bf16[1,16,2,8,256]{4,1,3,2,0:T(8,128)(2,1)S(1)}, u32[]{:S(2)}, u32[]{:S(2)}) %collective-permute-start.3) | collective-permute-done | bytes 131104 | tf_op jit(solution)/shard_map/ppermute | solution.py:22
  41.8 8.4 %collective-permute-start.4 = (bf16[1,16,2,8,256]{4,1,3,2,0:T(8,128)(2,1)S(1)}, bf16[1,16,2,8,256]{4,1,3,2,0:T(8,128)(2,1)S(1)}, u32[]{:S(2)}, u32[]{:S(2)}) collective-permute-start(bf16[1,16,2,8,256]{4,1,3,2,0:T(8,128)(2,1)S(1)} %broadcast_select_fusion.2), channel_id=1, source_target_pairs={{0,16},{16,0},{1,17},{17,1},{2,18},{18,2},{3,19},{19,3},{4,20},{20... | collective-permute-start | bytes 393224 | tf_op jit(solution)/shard_map/ppermute | solution.py:22
  50.3 2.4 collective-permute-done.4
  52.7 7.5 %collective-permute-start.5 = (bf16[1,16,2,8,256]{4,1,3,2,0:T(8,128)(2,1)S(1)}, bf16[1,16,2,8,256]{4,1,3,2,0:T(8,128)(2,1)S(1)}, u32[]{:S(2)}, u32[]{:S(2)}) collective-permute-start(bf16[1,16,2,8,256]{4,1,3,2,0:T(8,128)(2,1)S(1)} %broadcast_select_fusion.1), channel_id=1, source_target_pairs={{0,32},{32,0},{1,33},{33,1},{2,34},{34,2},{3,35},{35,3},{4,36},{36... | collective-permute-start | bytes 393224 | tf_op jit(solution)/shard_map/ppermute | solution.py:22
  60.2 2.4 collective-permute-done.5
  62.6 3.1 collective-permute-start.6
  67.7 15.7 %collective-permute-done.6 = bf16[1,16,2,8,256]{4,1,3,2,0:T(8,128)(2,1)S(1)} collective-permute-done((bf16[1,16,2,8,256]{4,1,3,2,0:T(8,128)(2,1)S(1)}, bf16[1,16,2,8,256]{4,1,3,2,0:T(8,128)(2,1)S(1)}, u32[]{:S(2)}, u32[]{:S(2)}) %collective-permute-start.6) | collective-permute-done | bytes 131104 | tf_op jit(solution)/shard_map/ppermute | solution.py:28
  83.4 1.9 collective-permute-start.7
  85.4 12.2 %collective-permute-done.7 = bf16[1,16,2,8,256]{4,1,3,2,0:T(8,128)(2,1)S(1)} collective-permute-done((bf16[1,16,2,8,256]{4,1,3,2,0:T(8,128)(2,1)S(1)}, bf16[1,16,2,8,256]{4,1,3,2,0:T(8,128)(2,1)S(1)}, u32[]{:S(2)}, u32[]{:S(2)}) %collective-permute-start.7) | collective-permute-done | bytes 131104 | tf_op jit(solution)/shard_map/ppermute | solution.py:28
  97.6 1.9 collective-permute-start.8
  99.5 9.8 %collective-permute-done.8 = bf16[1,16,2,8,256]{4,1,3,2,0:T(8,128)(2,1)S(1)} collective-permute-done((bf16[1,16,2,8,256]{4,1,3,2,0:T(8,128)(2,1)S(1)}, bf16[1,16,2,8,256]{4,1,3,2,0:T(8,128)(2,1)S(1)}, u32[]{:S(2)}, u32[]{:S(2)}) %collective-permute-start.8) | collective-permute-done | bytes 131104 | tf_op jit(solution)/shard_map/ppermute | solution.py:28
  109.3 1.9 collective-permute-start.9
  111.3 10.7 %collective-permute-done.9 = bf16[1,16,2,8,256]{4,1,3,2,0:T(8,128)(2,1)S(1)} collective-permute-done((bf16[1,16,2,8,256]{4,1,3,2,0:T(8,128)(2,1)S(1)}, bf16[1,16,2,8,256]{4,1,3,2,0:T(8,128)(2,1)S(1)}, u32[]{:S(2)}, u32[]{:S(2)}) %collective-permute-start.9) | collective-permute-done | bytes 131104 | tf_op jit(solution)/shard_map/ppermute | solution.py:28
  122.0 1.9 collective-permute-start.10
  124.0 12.4 %collective-permute-done.10 = bf16[1,16,2,8,256]{4,1,3,2,0:T(8,128)(2,1)S(1)} collective-permute-done((bf16[1,16,2,8,256]{4,1,3,2,0:T(8,128)(2,1)S(1)}, bf16[1,16,2,8,256]{4,1,3,2,0:T(8,128)(2,1)S(1)}, u32[]{:S(2)}, u32[]{:S(2)}) %collective-permute-start.10) | collective-permute-done | bytes 131104 | tf_op jit(solution)/shard_map/ppermute | solution.py:28
  136.4 8.2 %collective-permute-start.11 = (bf16[1,16,2,8,256]{4,1,3,2,0:T(8,128)(2,1)S(1)}, bf16[1,16,2,8,256]{4,1,3,2,0:T(8,128)(2,1)S(1)}, u32[]{:S(2)}, u32[]{:S(2)}) collective-permute-start(bf16[1,16,2,8,256]{4,1,3,2,0:T(8,128)(2,1)S(1)} %broadcast_select_fusion.10), channel_id=1, source_target_pairs={{0,32},{1,33},{2,34},{3,35},{4,36},{5,37},{6,38},{7,39},{8,40},{9,... | collective-permute-start | bytes 393224 | tf_op jit(solution)/shard_map/ppermute | solution.py:28
  146.3 0.7 collective-permute-done.11
  147.0 1.9 collective-permute-start.12
  148.9 0.4 fusion.386
  152.8 8.1 %collective-permute-done.12 = bf16[1,16,2,8,256]{4,1,3,2,0:T(8,128)(2,1)S(1)} collective-permute-done((bf16[1,16,2,8,256]{4,1,3,2,0:T(8,128)(2,1)S(1)}, bf16[1,16,2,8,256]{4,1,3,2,0:T(8,128)(2,1)S(1)}, u32[]{:S(2)}, u32[]{:S(2)}) %collective-permute-start.12) | collective-permute-done | bytes 131104 | tf_op jit(solution)/shard_map/ppermute | solution.py:28
  160.9 1.9 collective-permute-start.13
  162.8 11.5 %collective-permute-start.14 = (bf16[1,16,1,8,256]{4,1,3,2,0:T(8,128)(2,1)S(1)}, bf16[1,16,1,8,256]{4,1,3,2,0:T(8,128)(2,1)S(1)}, u32[]{:S(2)}, u32[]{:S(2)}) collective-permute-start(bf16[1,16,1,8,256]{4,1,3,2,0:T(8,128)(2,1)S(1)} %get-tuple-element.128), channel_id=1, source_target_pairs={{1,0},{2,1},{3,2},{4,3},{5,4},{6,5},{7,6},{8,7},{9,8},{10,9},{11,1... | collective-permute-start | bytes 196616 | tf_op jit(solution)/shard_map/ppermute | solution.py:39
  174.5 1.1 collective-permute-done.14
  182.3 0.7 convert_reduce_fusion
  183.7 0.3 fusion.65
  184.4 0.3 fusion.62
  185.1 0.3 fusion.59
  185.8 0.3 fusion.56
  186.5 0.3 fusion.53
  187.2 0.3 fusion.50
  187.9 0.3 fusion.47
  188.6 0.3 fusion.44
  189.3 122.1 %all-reduce = (f32[27,16,16]{2,1,0:T(8,128)S(1)}, f32[16]{0:T(128)S(1)}) all-reduce(f32[27,16,16]{2,1,0:T(8,128)S(1)} %fusion.42, f32[16]{0:T(128)S(1)} %get-tuple-element.25), channel_id=1, replica_groups=mesh['dp'=8,'gx'=64] {'dp','gx'}, use_global_device_ids=true, to_apply=%region_0.1 | all-reduce | flops 6928 | bytes 55424 | tf_op jit(solution)/shard_map/psum | solution.py:122
  311.4 5.0 %collective-permute-start.15 = (bf16[1,16,1,8,256]{4,1,3,2,0:T(8,128)(2,1)S(1)}, bf16[1,16,1,8,256]{4,1,3,2,0:T(8,128)(2,1)S(1)}, u32[]{:S(2)}, u32[]{:S(2)}) collective-permute-start(bf16[1,16,1,8,256]{4,1,3,2,0:T(8,128)(2,1)S(1)} %get-tuple-element.95), channel_id=1, source_target_pairs={{1,0},{2,1},{3,2},{4,3},{5,4},{6,5},{7,6},{8,7},{9,8},{10,9},{11,1... | collective-permute-start | bytes 196616 | tf_op jit(solution)/shard_map/ppermute | solution.py:39
  316.4 1.9 collective-permute-start.16
  318.3 0.5 broadcast_multiply_fusion.1
  318.8 0.8 copy.128
  319.6 0.7 copy.126
  320.3 9.7 %collective-permute-done.16 = bf16[1,16,1,8,256]{4,1,3,2,0:T(8,128)(2,1)S(1)} collective-permute-done((bf16[1,16,1,8,256]{4,1,3,2,0:T(8,128)(2,1)S(1)}, bf16[1,16,1,8,256]{4,1,3,2,0:T(8,128)(2,1)S(1)}, u32[]{:S(2)}, u32[]{:S(2)}) %collective-permute-start.16) | collective-permute-done | bytes 65568 | tf_op jit(solution)/shard_map/ppermute | solution.py:38
  332.3 0.3 convolution_add_fusion.13
  333.4 0.3 convolution_add_fusion.10
  334.1 0.3 convolution_add_fusion.7
  334.9 0.3 convolution_add_fusion.4
  337.4 0.3 convolution_add_fusion.1
  337.9 0.3 fusion.7
  338.2 0.3 fusion.41
  338.5 0.7 copy.127
  (154 shorter events, 22.5 us)
Async XLA Ops:
  0.6 7.4 %copy-start = (bf16[1,16,2,8,256]{4,3,2,1,0:T(8,128)(2,1)S(1)}, bf16[1,16,2,8,256]{4,3,2,1,0:T(8,128)(2,1)}, u32[]{:S(2)}) copy-start(bf16[1,16,2,8,256]{4,3,2,1,0:T(8,128)(2,1)} %param.6) | copy-start | bytes 393220
  11.5 6.3 %collective-permute-start = (bf16[1,16,2,8,256]{4,1,3,2,0:T(8,128)(2,1)S(1)}, bf16[1,16,2,8,256]{4,1,3,2,0:T(8,128)(2,1)S(1)}, u32[]{:S(2)}, u32[]{:S(2)}) collective-permute-start(bf16[1,16,2,8,256]{4,1,3,2,0:T(8,128)(2,1)S(1)} %reverse_select_fusion), channel_id=1, source_target_pairs={{0,1},{1,0},{2,3},{3,2},{4,5},{5,4},{6,7},{7,6},{8,9},{9,8},{10,11... | collective-permute-start | bytes 393224 | tf_op jit(solution)/shard_map/ppermute | solution.py:22
  17.8 7.8 %collective-permute-start.1 = (bf16[1,16,2,8,256]{4,1,3,2,0:T(8,128)(2,1)S(1)}, bf16[1,16,2,8,256]{4,1,3,2,0:T(8,128)(2,1)S(1)}, u32[]{:S(2)}, u32[]{:S(2)}) collective-permute-start(bf16[1,16,2,8,256]{4,1,3,2,0:T(8,128)(2,1)S(1)} %broadcast_select_fusion.5), channel_id=1, source_target_pairs={{0,2},{2,0},{1,3},{3,1},{4,6},{6,4},{5,7},{7,5},{8,10},{10,8},{9,1... | collective-permute-start | bytes 393224 | tf_op jit(solution)/shard_map/ppermute | solution.py:22
  25.6 6.9 %collective-permute-start.2 = (bf16[1,16,2,8,256]{4,1,3,2,0:T(8,128)(2,1)S(1)}, bf16[1,16,2,8,256]{4,1,3,2,0:T(8,128)(2,1)S(1)}, u32[]{:S(2)}, u32[]{:S(2)}) collective-permute-start(bf16[1,16,2,8,256]{4,1,3,2,0:T(8,128)(2,1)S(1)} %broadcast_select_fusion.4), channel_id=1, source_target_pairs={{0,4},{4,0},{1,5},{5,1},{2,6},{6,2},{3,7},{7,3},{8,12},{12,8},{9,1... | collective-permute-start | bytes 393224 | tf_op jit(solution)/shard_map/ppermute | solution.py:22
  32.5 9.3 %collective-permute-start.3 = (bf16[1,16,2,8,256]{4,1,3,2,0:T(8,128)(2,1)S(1)}, bf16[1,16,2,8,256]{4,1,3,2,0:T(8,128)(2,1)S(1)}, u32[]{:S(2)}, u32[]{:S(2)}) collective-permute-start(bf16[1,16,2,8,256]{4,1,3,2,0:T(8,128)(2,1)S(1)} %broadcast_select_fusion.3), channel_id=1, source_target_pairs={{0,8},{8,0},{1,9},{9,1},{2,10},{10,2},{3,11},{11,3},{4,12},{12,4},... | collective-permute-start | bytes 393224 | tf_op jit(solution)/shard_map/ppermute | solution.py:22
  41.8 10.9 %collective-permute-start.4 = (bf16[1,16,2,8,256]{4,1,3,2,0:T(8,128)(2,1)S(1)}, bf16[1,16,2,8,256]{4,1,3,2,0:T(8,128)(2,1)S(1)}, u32[]{:S(2)}, u32[]{:S(2)}) collective-permute-start(bf16[1,16,2,8,256]{4,1,3,2,0:T(8,128)(2,1)S(1)} %broadcast_select_fusion.2), channel_id=1, source_target_pairs={{0,16},{16,0},{1,17},{17,1},{2,18},{18,2},{3,19},{19,3},{4,20},{20... | collective-permute-start | bytes 393224 | tf_op jit(solution)/shard_map/ppermute | solution.py:22
  52.7 9.9 %collective-permute-start.5 = (bf16[1,16,2,8,256]{4,1,3,2,0:T(8,128)(2,1)S(1)}, bf16[1,16,2,8,256]{4,1,3,2,0:T(8,128)(2,1)S(1)}, u32[]{:S(2)}, u32[]{:S(2)}) collective-permute-start(bf16[1,16,2,8,256]{4,1,3,2,0:T(8,128)(2,1)S(1)} %broadcast_select_fusion.1), channel_id=1, source_target_pairs={{0,32},{32,0},{1,33},{33,1},{2,34},{34,2},{3,35},{35,3},{4,36},{36... | collective-permute-start | bytes 393224 | tf_op jit(solution)/shard_map/ppermute | solution.py:22
  62.6 20.8 %collective-permute-start.6 = (bf16[1,16,2,8,256]{4,1,3,2,0:T(8,128)(2,1)S(1)}, bf16[1,16,2,8,256]{4,1,3,2,0:T(8,128)(2,1)S(1)}, u32[]{:S(2)}, u32[]{:S(2)}) collective-permute-start(bf16[1,16,2,8,256]{4,1,3,2,0:T(8,128)(2,1)S(1)} %broadcast_select_fusion), channel_id=1, source_target_pairs={{0,1},{1,2},{2,3},{3,4},{4,5},{5,6},{6,7},{7,8},{8,9},{9,10},{10,1... | collective-permute-start | bytes 393224 | tf_op jit(solution)/shard_map/ppermute | solution.py:28
  83.4 61.2 %copy-start.1 = (bf16[27,16,16]{0,2,1:T(8,128)(2,1)S(1)}, bf16[27,16,16]{0,2,1:T(8,128)(2,1)}, u32[]{:S(2)}) copy-start(bf16[27,16,16]{0,2,1:T(8,128)(2,1)} %param.9) | copy-start | bytes 41476
  83.4 14.1 %collective-permute-start.7 = (bf16[1,16,2,8,256]{4,1,3,2,0:T(8,128)(2,1)S(1)}, bf16[1,16,2,8,256]{4,1,3,2,0:T(8,128)(2,1)S(1)}, u32[]{:S(2)}, u32[]{:S(2)}) collective-permute-start(bf16[1,16,2,8,256]{4,1,3,2,0:T(8,128)(2,1)S(1)} %broadcast_select_fusion.6), channel_id=1, source_target_pairs={{0,2},{1,3},{2,4},{3,5},{4,6},{5,7},{6,8},{7,9},{8,10},{9,11},{10,... | collective-permute-start | bytes 393224 | tf_op jit(solution)/shard_map/ppermute | solution.py:28
  97.6 11.7 %collective-permute-start.8 = (bf16[1,16,2,8,256]{4,1,3,2,0:T(8,128)(2,1)S(1)}, bf16[1,16,2,8,256]{4,1,3,2,0:T(8,128)(2,1)S(1)}, u32[]{:S(2)}, u32[]{:S(2)}) collective-permute-start(bf16[1,16,2,8,256]{4,1,3,2,0:T(8,128)(2,1)S(1)} %broadcast_select_fusion.7), channel_id=1, source_target_pairs={{0,4},{1,5},{2,6},{3,7},{4,8},{5,9},{6,10},{7,11},{8,12},{9,13},{1... | collective-permute-start | bytes 393224 | tf_op jit(solution)/shard_map/ppermute | solution.py:28
  109.3 12.6 %collective-permute-start.9 = (bf16[1,16,2,8,256]{4,1,3,2,0:T(8,128)(2,1)S(1)}, bf16[1,16,2,8,256]{4,1,3,2,0:T(8,128)(2,1)S(1)}, u32[]{:S(2)}, u32[]{:S(2)}) collective-permute-start(bf16[1,16,2,8,256]{4,1,3,2,0:T(8,128)(2,1)S(1)} %broadcast_select_fusion.8), channel_id=1, source_target_pairs={{0,8},{1,9},{2,10},{3,11},{4,12},{5,13},{6,14},{7,15},{8,16},{9,17... | collective-permute-start | bytes 393224 | tf_op jit(solution)/shard_map/ppermute | solution.py:28
  122.0 14.4 %collective-permute-start.10 = (bf16[1,16,2,8,256]{4,1,3,2,0:T(8,128)(2,1)S(1)}, bf16[1,16,2,8,256]{4,1,3,2,0:T(8,128)(2,1)S(1)}, u32[]{:S(2)}, u32[]{:S(2)}) collective-permute-start(bf16[1,16,2,8,256]{4,1,3,2,0:T(8,128)(2,1)S(1)} %broadcast_select_fusion.9), channel_id=1, source_target_pairs={{0,16},{1,17},{2,18},{3,19},{4,20},{5,21},{6,22},{7,23},{8,24},{9,... | collective-permute-start | bytes 393224 | tf_op jit(solution)/shard_map/ppermute | solution.py:28
  136.4 10.5 %collective-permute-start.11 = (bf16[1,16,2,8,256]{4,1,3,2,0:T(8,128)(2,1)S(1)}, bf16[1,16,2,8,256]{4,1,3,2,0:T(8,128)(2,1)S(1)}, u32[]{:S(2)}, u32[]{:S(2)}) collective-permute-start(bf16[1,16,2,8,256]{4,1,3,2,0:T(8,128)(2,1)S(1)} %broadcast_select_fusion.10), channel_id=1, source_target_pairs={{0,32},{1,33},{2,34},{3,35},{4,36},{5,37},{6,38},{7,39},{8,40},{9,... | collective-permute-start | bytes 393224 | tf_op jit(solution)/shard_map/ppermute | solution.py:28
  147.0 13.8 %collective-permute-start.12 = (bf16[1,16,2,8,256]{4,1,3,2,0:T(8,128)(2,1)S(1)}, bf16[1,16,2,8,256]{4,1,3,2,0:T(8,128)(2,1)S(1)}, u32[]{:S(2)}, u32[]{:S(2)}) collective-permute-start(bf16[1,16,2,8,256]{4,1,3,2,0:T(8,128)(2,1)S(1)} %broadcast_select_fusion.11), channel_id=1, source_target_pairs={{0,1},{1,2},{2,3},{3,4},{4,5},{5,6},{6,7},{7,8},{8,9},{9,10},{10,1... | collective-permute-start | bytes 393224 | tf_op jit(solution)/shard_map/ppermute | solution.py:28
  160.9 13.6 %collective-permute-start.13 = (bf16[1,16,1,8,256]{4,1,3,2,0:T(8,128)(2,1)S(1)}, bf16[1,16,1,8,256]{4,1,3,2,0:T(8,128)(2,1)S(1)}, u32[]{:S(2)}, u32[]{:S(2)}) collective-permute-start(bf16[1,16,1,8,256]{4,1,3,2,0:T(8,128)(2,1)S(1)} %get-tuple-element.127), channel_id=1, source_target_pairs={{0,1},{1,2},{2,3},{3,4},{4,5},{5,6},{6,7},{7,8},{8,9},{9,10},{10,1... | collective-permute-start | bytes 196616 | tf_op jit(solution)/shard_map/ppermute | solution.py:38
  162.8 12.8 %collective-permute-start.14 = (bf16[1,16,1,8,256]{4,1,3,2,0:T(8,128)(2,1)S(1)}, bf16[1,16,1,8,256]{4,1,3,2,0:T(8,128)(2,1)S(1)}, u32[]{:S(2)}, u32[]{:S(2)}) collective-permute-start(bf16[1,16,1,8,256]{4,1,3,2,0:T(8,128)(2,1)S(1)} %get-tuple-element.128), channel_id=1, source_target_pairs={{1,0},{2,1},{3,2},{4,3},{5,4},{6,5},{7,6},{8,7},{9,8},{10,9},{11,1... | collective-permute-start | bytes 196616 | tf_op jit(solution)/shard_map/ppermute | solution.py:39
  180.8 1.0 copy-start.3
  181.3 1.1 copy-start.2
  311.4 9.0 %collective-permute-start.15 = (bf16[1,16,1,8,256]{4,1,3,2,0:T(8,128)(2,1)S(1)}, bf16[1,16,1,8,256]{4,1,3,2,0:T(8,128)(2,1)S(1)}, u32[]{:S(2)}, u32[]{:S(2)}) collective-permute-start(bf16[1,16,1,8,256]{4,1,3,2,0:T(8,128)(2,1)S(1)} %get-tuple-element.95), channel_id=1, source_target_pairs={{1,0},{2,1},{3,2},{4,3},{5,4},{6,5},{7,6},{8,7},{9,8},{10,9},{11,1... | collective-permute-start | bytes 196616 | tf_op jit(solution)/shard_map/ppermute | solution.py:39
  316.4 13.7 %collective-permute-start.16 = (bf16[1,16,1,8,256]{4,1,3,2,0:T(8,128)(2,1)S(1)}, bf16[1,16,1,8,256]{4,1,3,2,0:T(8,128)(2,1)S(1)}, u32[]{:S(2)}, u32[]{:S(2)}) collective-permute-start(bf16[1,16,1,8,256]{4,1,3,2,0:T(8,128)(2,1)S(1)} %get-tuple-element.96), channel_id=1, source_target_pairs={{0,1},{1,2},{2,3},{3,4},{4,5},{5,6},{6,7},{7,8},{8,9},{9,10},{10,1... | collective-permute-start | bytes 196616 | tf_op jit(solution)/shard_map/ppermute | solution.py:38
where the time goes:
time: 340 us; the launch traced here: 339 us
  blocking collectives  122 us (36%)
  waiting for transfers between devices  96.3 us (28%)
  starting transfers between devices  76.2 us (22%)
  matrix products  18.9 us (6%)
  local copies, waits for them, and re-layouts  14.7 us (4%)
  between operations  5.71 us (2%)
  other arithmetic  5.36 us (2%)
    psum x1, blocking collectives, on_device(): summed_w, summed_b = lax.psum((jnp.stack(grad_list), grad_b), ('dp', 'gx'))  122 us
    ppermute x7, waiting for transfers between devices, shifted(): return lax.ppermute(value, axis, pairs)  69.4 us
    ppermute x6, starting transfers between devices, partner_2(): return lax.ppermute(block, axis, route)  35 us
    ppermute x7, starting transfers between devices, shifted(): return lax.ppermute(value, axis, pairs)  20.9 us
    ppermute x2, starting transfers between devices, padded_2(): after = lax.ppermute(leading, axis, down)  16.5 us
    ppermute x6, waiting for transfers between devices, partner_2(): return lax.ppermute(block, axis, route)  16 us
    ppermute x2, waiting for transfers between devices, padded_2(): before = lax.ppermute(last, axis, up)  9.7 us
    unnamed x38, local copies, waits for them, and re-layouts  7.13 us
  transfers between devices with their start and end apart: 17, of which 15 were waited for; matrix products, arithmetic and copies ran while one was open for 2% of the time, Pallas kernels for 0%

commit v1 on v0

--- a/solution.py
+++ b/solution.py
@@ -119,7 +119,7 @@
             "oi,boxyz->bixyz", weight[tap_index], moved_grad, preferred_element_type=jnp.float32
         )
     grad_b = jnp.sum(grad_pre.astype(jnp.float32), axis=(0, 2, 3, 4))
-    summed_w, summed_b = lax.psum((jnp.stack(grad_list), grad_b), ("dp", "gx"))
+    summed_w, summed_b = lax.psum(lax.psum((jnp.stack(grad_list), grad_b), "dp"), "gx")
     cell_count = (
         features.shape[0] * lax.axis_size("dp") * length_x * features.shape[3] * features.shape[4]
     )

time: 340 us -> 701 us (2.06)
  the two profiles are of different devices: /device:TPU:1 before, /device:TPU:32 now
where the time goes in v1:
time: 701 us; the launch traced here: 700 us
  blocking collectives  467 us (67%)
  waiting for transfers between devices  117 us (17%)
  starting transfers between devices  70.8 us (10%)
  matrix products  18.9 us (3%)
  local copies, waits for them, and re-layouts  14.7 us (2%)
    psum x1, blocking collectives, on_device(): lax.psum(lax.psum((jnp.stack(grad_list), grad_b), 'dp'), 'gx')  438 us
    ppermute x7, waiting for transfers between devices, shifted(): return lax.ppermute(value, axis, pairs)  83.6 us
    ppermute x6, starting transfers between devices, partner_2(): return lax.ppermute(block, axis, route)  33.6 us
    psum x1, blocking collectives, on_device(): lax.psum((jnp.stack(grad_list), grad_b), 'dp')  28.9 us
    ppermute x6, waiting for transfers between devices, partner_2(): return lax.ppermute(block, axis, route)  23.8 us
    ppermute x7, starting transfers between devices, shifted(): return lax.ppermute(value, axis, pairs)  17.4 us
  transfers between devices with their start and end apart: 17, of which 16 were waited for; matrix products, arithmetic and copies ran while one was open for 1% of the time, Pallas kernels for 0%

profile of v1, /device:TPU:32, one launch (start us, length us, event | category | flops | bytes accessed | tf_op | source)
XLA Modules:
  0.0 700.0 jit_solution(16162371456205259272)
XLA Ops:
  0.6 1.4 fusion.388
  2.1 1.4 fusion.389
  4.1 0.7 compare_and_fusion.1
  4.7 0.7 compare_select_fusion
  6.1 0.6 compare_select_fusion.4
  6.7 0.6 compare_and_fusion
  8.0 0.9 gather_fusion
  9.1 0.6 copy.69
  9.6 0.9 gather_fusion.1
  10.6 0.8 copy.70
  11.5 3.4 collective-permute-start
  14.9 3.7 collective-permute-done
  18.7 4.9 collective-permute-start.1
  23.6 3.4 collective-permute-done.1
  27.1 4.3 collective-permute-start.2
  31.3 2.9 collective-permute-done.2
  34.3 6.1 collective-permute-start.3
  40.4 2.9 collective-permute-done.3
  43.3 10.8 %collective-permute-start.4 = (bf16[1,16,2,8,256]{4,1,3,2,0:T(8,128)(2,1)S(1)}, bf16[1,16,2,8,256]{4,1,3,2,0:T(8,128)(2,1)S(1)}, u32[]{:S(2)}, u32[]{:S(2)}) collective-permute-start(bf16[1,16,2,8,256]{4,1,3,2,0:T(8,128)(2,1)S(1)} %broadcast_select_fusion.2), channel_id=1, source_target_pairs={{0,16},{16,0},{1,17},{17,1},{2,18},{18,2},{3,19},{19,3},{4,20},{20... | collective-permute-start | bytes 393224 | tf_op jit(solution)/shard_map/ppermute | solution.py:22
  54.1 3.0 collective-permute-done.4
  57.1 4.1 collective-permute-start.5
  61.2 7.8 %collective-permute-done.5 = bf16[1,16,2,8,256]{4,1,3,2,0:T(8,128)(2,1)S(1)} collective-permute-done((bf16[1,16,2,8,256]{4,1,3,2,0:T(8,128)(2,1)S(1)}, bf16[1,16,2,8,256]{4,1,3,2,0:T(8,128)(2,1)S(1)}, u32[]{:S(2)}, u32[]{:S(2)}) %collective-permute-start.5) | collective-permute-done | bytes 131104 | tf_op jit(solution)/shard_map/ppermute | solution.py:22
  69.1 3.6 collective-permute-start.6
  74.7 13.3 %collective-permute-done.6 = bf16[1,16,2,8,256]{4,1,3,2,0:T(8,128)(2,1)S(1)} collective-permute-done((bf16[1,16,2,8,256]{4,1,3,2,0:T(8,128)(2,1)S(1)}, bf16[1,16,2,8,256]{4,1,3,2,0:T(8,128)(2,1)S(1)}, u32[]{:S(2)}, u32[]{:S(2)}) %collective-permute-start.6) | collective-permute-done | bytes 131104 | tf_op jit(solution)/shard_map/ppermute | solution.py:28
  88.0 1.9 collective-permute-start.7
  89.9 17.0 %collective-permute-done.7 = bf16[1,16,2,8,256]{4,1,3,2,0:T(8,128)(2,1)S(1)} collective-permute-done((bf16[1,16,2,8,256]{4,1,3,2,0:T(8,128)(2,1)S(1)}, bf16[1,16,2,8,256]{4,1,3,2,0:T(8,128)(2,1)S(1)}, u32[]{:S(2)}, u32[]{:S(2)}) %collective-permute-start.7) | collective-permute-done | bytes 131104 | tf_op jit(solution)/shard_map/ppermute | solution.py:28
  107.0 1.9 collective-permute-start.8
  109.0 12.3 %collective-permute-done.8 = bf16[1,16,2,8,256]{4,1,3,2,0:T(8,128)(2,1)S(1)} collective-permute-done((bf16[1,16,2,8,256]{4,1,3,2,0:T(8,128)(2,1)S(1)}, bf16[1,16,2,8,256]{4,1,3,2,0:T(8,128)(2,1)S(1)}, u32[]{:S(2)}, u32[]{:S(2)}) %collective-permute-start.8) | collective-permute-done | bytes 131104 | tf_op jit(solution)/shard_map/ppermute | solution.py:28
  121.3 1.9 collective-permute-start.9
  123.3 13.2 %collective-permute-done.9 = bf16[1,16,2,8,256]{4,1,3,2,0:T(8,128)(2,1)S(1)} collective-permute-done((bf16[1,16,2,8,256]{4,1,3,2,0:T(8,128)(2,1)S(1)}, bf16[1,16,2,8,256]{4,1,3,2,0:T(8,128)(2,1)S(1)}, u32[]{:S(2)}, u32[]{:S(2)}) %collective-permute-start.9) | collective-permute-done | bytes 131104 | tf_op jit(solution)/shard_map/ppermute | solution.py:28
  136.5 1.9 collective-permute-start.10
  138.5 13.6 %collective-permute-done.10 = bf16[1,16,2,8,256]{4,1,3,2,0:T(8,128)(2,1)S(1)} collective-permute-done((bf16[1,16,2,8,256]{4,1,3,2,0:T(8,128)(2,1)S(1)}, bf16[1,16,2,8,256]{4,1,3,2,0:T(8,128)(2,1)S(1)}, u32[]{:S(2)}, u32[]{:S(2)}) %collective-permute-start.10) | collective-permute-done | bytes 131104 | tf_op jit(solution)/shard_map/ppermute | solution.py:28
  152.1 4.2 collective-permute-start.11
  157.9 4.9 collective-permute-done.11
  162.9 1.9 collective-permute-start.12
  164.8 0.4 fusion.386
  168.7 9.2 %collective-permute-done.12 = bf16[1,16,2,8,256]{4,1,3,2,0:T(8,128)(2,1)S(1)} collective-permute-done((bf16[1,16,2,8,256]{4,1,3,2,0:T(8,128)(2,1)S(1)}, bf16[1,16,2,8,256]{4,1,3,2,0:T(8,128)(2,1)S(1)}, u32[]{:S(2)}, u32[]{:S(2)}) %collective-permute-start.12) | collective-permute-done | bytes 131104 | tf_op jit(solution)/shard_map/ppermute | solution.py:28
  178.0 1.9 collective-permute-start.13
  179.9 12.0 %collective-permute-start.14 = (bf16[1,16,1,8,256]{4,1,3,2,0:T(8,128)(2,1)S(1)}, bf16[1,16,1,8,256]{4,1,3,2,0:T(8,128)(2,1)S(1)}, u32[]{:S(2)}, u32[]{:S(2)}) collective-permute-start(bf16[1,16,1,8,256]{4,1,3,2,0:T(8,128)(2,1)S(1)} %get-tuple-element.130), channel_id=1, source_target_pairs={{1,0},{2,1},{3,2},{4,3},{5,4},{6,5},{7,6},{8,7},{9,8},{10,9},{11,1... | collective-permute-start | bytes 196616 | tf_op jit(solution)/shard_map/ppermute | solution.py:39
  192.3 1.6 collective-permute-done.14
  200.5 0.7 convert_reduce_fusion
  201.9 0.3 fusion.65
  202.6 0.3 fusion.62
  203.3 0.3 fusion.59
  204.0 0.3 fusion.56
  204.7 0.3 fusion.53
  205.4 0.3 fusion.50
  206.1 0.3 fusion.47
  207.5 28.9 %all-reduce.1 = (f32[27,16,16]{2,1,0:T(8,128)S(1)}, f32[16]{0:T(128)S(1)}) all-reduce(f32[27,16,16]{2,1,0:T(8,128)S(1)} %fusion.42, f32[16]{0:T(128)S(1)} %get-tuple-element.27), channel_id=1, replica_groups=mesh['dp'=8,'gx'=64] {'dp'}, use_global_device_ids=true, to_apply=%region_0.1 | all-reduce | flops 6928 | bytes 55424 | tf_op jit(solution)/shard_map/psum | solution.py:122
  236.3 438.3 %all-reduce = (f32[27,16,16]{2,1,0:T(8,128)S(1)}, f32[16]{0:T(128)S(1)}) all-reduce(f32[27,16,16]{2,1,0:T(8,128)S(1)} %get-tuple-element.25, f32[16]{0:T(128)S(1)} %get-tuple-element.26), channel_id=1, replica_groups=mesh['dp'=8,'gx'=64] {'gx'}, use_global_device_ids=true, to_apply=%region_1.2 | all-reduce | flops 6928 | bytes 55424 | tf_op jit(solution)/shard_map/psum | solution.py:122
  674.7 1.9 collective-permute-start.15
  676.6 3.9 collective-permute-start.16
  680.5 0.5 broadcast_multiply_fusion.1
  681.1 0.8 copy.128
  681.9 0.7 copy.126
  682.6 8.3 %collective-permute-done.16 = bf16[1,16,1,8,256]{4,1,3,2,0:T(8,128)(2,1)S(1)} collective-permute-done((bf16[1,16,1,8,256]{4,1,3,2,0:T(8,128)(2,1)S(1)}, bf16[1,16,1,8,256]{4,1,3,2,0:T(8,128)(2,1)S(1)}, u32[]{:S(2)}, u32[]{:S(2)}) %collective-permute-start.16) | collective-permute-done | bytes 65568 | tf_op jit(solution)/shard_map/ppermute | solution.py:38
  693.2 0.3 convolution_add_fusion.13
  694.2 0.3 convolution_add_fusion.10
  695.0 0.3 convolution_add_fusion.7
  695.7 0.3 convolution_add_fusion.4
  698.3 0.3 convolution_add_fusion.1
  698.8 0.3 fusion.7
  699.1 0.3 fusion.41
  699.3 0.7 copy.127
  (155 shorter events, 22.9 us)
Async XLA Ops:
  0.6 7.4 %copy-start = (bf16[1,16,2,8,256]{4,3,2,1,0:T(8,128)(2,1)S(1)}, bf16[1,16,2,8,256]{4,3,2,1,0:T(8,128)(2,1)}, u32[]{:S(2)}) copy-start(bf16[1,16,2,8,256]{4,3,2,1,0:T(8,128)(2,1)} %param.6) | copy-start | bytes 393220
  11.5 7.1 %collective-permute-start = (bf16[1,16,2,8,256]{4,1,3,2,0:T(8,128)(2,1)S(1)}, bf16[1,16,2,8,256]{4,1,3,2,0:T(8,128)(2,1)S(1)}, u32[]{:S(2)}, u32[]{:S(2)}) collective-permute-start(bf16[1,16,2,8,256]{4,1,3,2,0:T(8,128)(2,1)S(1)} %reverse_select_fusion), channel_id=1, source_target_pairs={{0,1},{1,0},{2,3},{3,2},{4,5},{5,4},{6,7},{7,6},{8,9},{9,8},{10,11... | collective-permute-start | bytes 393224 | tf_op jit(solution)/shard_map/ppermute | solution.py:22
  18.7 8.4 %collective-permute-start.1 = (bf16[1,16,2,8,256]{4,1,3,2,0:T(8,128)(2,1)S(1)}, bf16[1,16,2,8,256]{4,1,3,2,0:T(8,128)(2,1)S(1)}, u32[]{:S(2)}, u32[]{:S(2)}) collective-permute-start(bf16[1,16,2,8,256]{4,1,3,2,0:T(8,128)(2,1)S(1)} %broadcast_select_fusion.5), channel_id=1, source_target_pairs={{0,2},{2,0},{1,3},{3,1},{4,6},{6,4},{5,7},{7,5},{8,10},{10,8},{9,1... | collective-permute-start | bytes 393224 | tf_op jit(solution)/shard_map/ppermute | solution.py:22
  27.1 7.2 %collective-permute-start.2 = (bf16[1,16,2,8,256]{4,1,3,2,0:T(8,128)(2,1)S(1)}, bf16[1,16,2,8,256]{4,1,3,2,0:T(8,128)(2,1)S(1)}, u32[]{:S(2)}, u32[]{:S(2)}) collective-permute-start(bf16[1,16,2,8,256]{4,1,3,2,0:T(8,128)(2,1)S(1)} %broadcast_select_fusion.4), channel_id=1, source_target_pairs={{0,4},{4,0},{1,5},{5,1},{2,6},{6,2},{3,7},{7,3},{8,12},{12,8},{9,1... | collective-permute-start | bytes 393224 | tf_op jit(solution)/shard_map/ppermute | solution.py:22
  34.3 9.0 %collective-permute-start.3 = (bf16[1,16,2,8,256]{4,1,3,2,0:T(8,128)(2,1)S(1)}, bf16[1,16,2,8,256]{4,1,3,2,0:T(8,128)(2,1)S(1)}, u32[]{:S(2)}, u32[]{:S(2)}) collective-permute-start(bf16[1,16,2,8,256]{4,1,3,2,0:T(8,128)(2,1)S(1)} %broadcast_select_fusion.3), channel_id=1, source_target_pairs={{0,8},{8,0},{1,9},{9,1},{2,10},{10,2},{3,11},{11,3},{4,12},{12,4},... | collective-permute-start | bytes 393224 | tf_op jit(solution)/shard_map/ppermute | solution.py:22
  43.3 13.8 %collective-permute-start.4 = (bf16[1,16,2,8,256]{4,1,3,2,0:T(8,128)(2,1)S(1)}, bf16[1,16,2,8,256]{4,1,3,2,0:T(8,128)(2,1)S(1)}, u32[]{:S(2)}, u32[]{:S(2)}) collective-permute-start(bf16[1,16,2,8,256]{4,1,3,2,0:T(8,128)(2,1)S(1)} %broadcast_select_fusion.2), channel_id=1, source_target_pairs={{0,16},{16,0},{1,17},{17,1},{2,18},{18,2},{3,19},{19,3},{4,20},{20... | collective-permute-start | bytes 393224 | tf_op jit(solution)/shard_map/ppermute | solution.py:22
  57.1 11.9 %collective-permute-start.5 = (bf16[1,16,2,8,256]{4,1,3,2,0:T(8,128)(2,1)S(1)}, bf16[1,16,2,8,256]{4,1,3,2,0:T(8,128)(2,1)S(1)}, u32[]{:S(2)}, u32[]{:S(2)}) collective-permute-start(bf16[1,16,2,8,256]{4,1,3,2,0:T(8,128)(2,1)S(1)} %broadcast_select_fusion.1), channel_id=1, source_target_pairs={{0,32},{32,0},{1,33},{33,1},{2,34},{34,2},{3,35},{35,3},{4,36},{36... | collective-permute-start | bytes 393224 | tf_op jit(solution)/shard_map/ppermute | solution.py:22
  69.1 18.9 %collective-permute-start.6 = (bf16[1,16,2,8,256]{4,1,3,2,0:T(8,128)(2,1)S(1)}, bf16[1,16,2,8,256]{4,1,3,2,0:T(8,128)(2,1)S(1)}, u32[]{:S(2)}, u32[]{:S(2)}) collective-permute-start(bf16[1,16,2,8,256]{4,1,3,2,0:T(8,128)(2,1)S(1)} %broadcast_select_fusion), channel_id=1, source_target_pairs={{0,1},{1,2},{2,3},{3,4},{4,5},{5,6},{6,7},{7,8},{8,9},{9,10},{10,1... | collective-permute-start | bytes 393224 | tf_op jit(solution)/shard_map/ppermute | solution.py:28
  87.9 68.3 %copy-start.1 = (bf16[27,16,16]{0,2,1:T(8,128)(2,1)S(1)}, bf16[27,16,16]{0,2,1:T(8,128)(2,1)}, u32[]{:S(2)}) copy-start(bf16[27,16,16]{0,2,1:T(8,128)(2,1)} %param.9) | copy-start | bytes 41476
  88.0 19.0 %collective-permute-start.7 = (bf16[1,16,2,8,256]{4,1,3,2,0:T(8,128)(2,1)S(1)}, bf16[1,16,2,8,256]{4,1,3,2,0:T(8,128)(2,1)S(1)}, u32[]{:S(2)}, u32[]{:S(2)}) collective-permute-start(bf16[1,16,2,8,256]{4,1,3,2,0:T(8,128)(2,1)S(1)} %broadcast_select_fusion.6), channel_id=1, source_target_pairs={{0,2},{1,3},{2,4},{3,5},{4,6},{5,7},{6,8},{7,9},{8,10},{9,11},{10,... | collective-permute-start | bytes 393224 | tf_op jit(solution)/shard_map/ppermute | solution.py:28
  107.0 14.3 %collective-permute-start.8 = (bf16[1,16,2,8,256]{4,1,3,2,0:T(8,128)(2,1)S(1)}, bf16[1,16,2,8,256]{4,1,3,2,0:T(8,128)(2,1)S(1)}, u32[]{:S(2)}, u32[]{:S(2)}) collective-permute-start(bf16[1,16,2,8,256]{4,1,3,2,0:T(8,128)(2,1)S(1)} %broadcast_select_fusion.7), channel_id=1, source_target_pairs={{0,4},{1,5},{2,6},{3,7},{4,8},{5,9},{6,10},{7,11},{8,12},{9,13},{1... | collective-permute-start | bytes 393224 | tf_op jit(solution)/shard_map/ppermute | solution.py:28
  121.3 15.2 %collective-permute-start.9 = (bf16[1,16,2,8,256]{4,1,3,2,0:T(8,128)(2,1)S(1)}, bf16[1,16,2,8,256]{4,1,3,2,0:T(8,128)(2,1)S(1)}, u32[]{:S(2)}, u32[]{:S(2)}) collective-permute-start(bf16[1,16,2,8,256]{4,1,3,2,0:T(8,128)(2,1)S(1)} %broadcast_select_fusion.8), channel_id=1, source_target_pairs={{0,8},{1,9},{2,10},{3,11},{4,12},{5,13},{6,14},{7,15},{8,16},{9,17... | collective-permute-start | bytes 393224 | tf_op jit(solution)/shard_map/ppermute | solution.py:28
  136.5 15.6 %collective-permute-start.10 = (bf16[1,16,2,8,256]{4,1,3,2,0:T(8,128)(2,1)S(1)}, bf16[1,16,2,8,256]{4,1,3,2,0:T(8,128)(2,1)S(1)}, u32[]{:S(2)}, u32[]{:S(2)}) collective-permute-start(bf16[1,16,2,8,256]{4,1,3,2,0:T(8,128)(2,1)S(1)} %broadcast_select_fusion.9), channel_id=1, source_target_pairs={{0,16},{1,17},{2,18},{3,19},{4,20},{5,21},{6,22},{7,23},{8,24},{9,... | collective-permute-start | bytes 393224 | tf_op jit(solution)/shard_map/ppermute | solution.py:28
  152.1 10.8 %collective-permute-start.11 = (bf16[1,16,2,8,256]{4,1,3,2,0:T(8,128)(2,1)S(1)}, bf16[1,16,2,8,256]{4,1,3,2,0:T(8,128)(2,1)S(1)}, u32[]{:S(2)}, u32[]{:S(2)}) collective-permute-start(bf16[1,16,2,8,256]{4,1,3,2,0:T(8,128)(2,1)S(1)} %broadcast_select_fusion.10), channel_id=1, source_target_pairs={{0,32},{1,33},{2,34},{3,35},{4,36},{5,37},{6,38},{7,39},{8,40},{9,... | collective-permute-start | bytes 393224 | tf_op jit(solution)/shard_map/ppermute | solution.py:28
  162.9 15.0 %collective-permute-start.12 = (bf16[1,16,2,8,256]{4,1,3,2,0:T(8,128)(2,1)S(1)}, bf16[1,16,2,8,256]{4,1,3,2,0:T(8,128)(2,1)S(1)}, u32[]{:S(2)}, u32[]{:S(2)}) collective-permute-start(bf16[1,16,2,8,256]{4,1,3,2,0:T(8,128)(2,1)S(1)} %broadcast_select_fusion.11), channel_id=1, source_target_pairs={{0,1},{1,2},{2,3},{3,4},{4,5},{5,6},{6,7},{7,8},{8,9},{9,10},{10,1... | collective-permute-start | bytes 393224 | tf_op jit(solution)/shard_map/ppermute | solution.py:28
  178.0 14.3 %collective-permute-start.13 = (bf16[1,16,1,8,256]{4,1,3,2,0:T(8,128)(2,1)S(1)}, bf16[1,16,1,8,256]{4,1,3,2,0:T(8,128)(2,1)S(1)}, u32[]{:S(2)}, u32[]{:S(2)}) collective-permute-start(bf16[1,16,1,8,256]{4,1,3,2,0:T(8,128)(2,1)S(1)} %get-tuple-element.129), channel_id=1, source_target_pairs={{0,1},{1,2},{2,3},{3,4},{4,5},{5,6},{6,7},{7,8},{8,9},{9,10},{10,1... | collective-permute-start | bytes 196616 | tf_op jit(solution)/shard_map/ppermute | solution.py:38
  179.9 13.9 %collective-permute-start.14 = (bf16[1,16,1,8,256]{4,1,3,2,0:T(8,128)(2,1)S(1)}, bf16[1,16,1,8,256]{4,1,3,2,0:T(8,128)(2,1)S(1)}, u32[]{:S(2)}, u32[]{:S(2)}) collective-permute-start(bf16[1,16,1,8,256]{4,1,3,2,0:T(8,128)(2,1)S(1)} %get-tuple-element.130), channel_id=1, source_target_pairs={{1,0},{2,1},{3,2},{4,3},{5,4},{6,5},{7,6},{8,7},{9,8},{10,9},{11,1... | collective-permute-start | bytes 196616 | tf_op jit(solution)/shard_map/ppermute | solution.py:39
  199.0 1.0 copy-start.3
  199.5 1.1 copy-start.2
  674.7 7.9 %collective-permute-start.15 = (bf16[1,16,1,8,256]{4,1,3,2,0:T(8,128)(2,1)S(1)}, bf16[1,16,1,8,256]{4,1,3,2,0:T(8,128)(2,1)S(1)}, u32[]{:S(2)}, u32[]{:S(2)}) collective-permute-start(bf16[1,16,1,8,256]{4,1,3,2,0:T(8,128)(2,1)S(1)} %get-tuple-element.97), channel_id=1, source_target_pairs={{1,0},{2,1},{3,2},{4,3},{5,4},{6,5},{7,6},{8,7},{9,8},{10,9},{11,1... | collective-permute-start | bytes 196616 | tf_op jit(solution)/shard_map/ppermute | solution.py:39
  676.6 14.3 %collective-permute-start.16 = (bf16[1,16,1,8,256]{4,1,3,2,0:T(8,128)(2,1)S(1)}, bf16[1,16,1,8,256]{4,1,3,2,0:T(8,128)(2,1)S(1)}, u32[]{:S(2)}, u32[]{:S(2)}) collective-permute-start(bf16[1,16,1,8,256]{4,1,3,2,0:T(8,128)(2,1)S(1)} %get-tuple-element.98), channel_id=1, source_target_pairs={{0,1},{1,2},{2,3},{3,4},{4,5},{5,6},{6,7},{7,8},{8,9},{9,10},{10,1... | collective-permute-start | bytes 196616 | tf_op jit(solution)/shard_map/ppermute | solution.py:38
